TPU v7x, 256 devices: a whole 4x4x8 slice. The times are simulated.
256 devices in a mesh: grp: 32 (over z, x), tp: 8 (over y, core).
Axes of the slice: x: 4, y: 4, z: 8, core: 2. Of those that a mesh axis runs over, the one named last changes fastest.
Arguments:
- tokens: bfloat16 [32768, 2048], P('grp'), may hold values from -6 to 6
- norm_gain: float32 [2048], replicated, may hold values from 0.5 to 7
- w_qkv: bfloat16 [2048, 3, 2048], P(None, None, 'tp'), may hold values from -0.125 to 0.125
- w_out: bfloat16 [2048, 2048], P('tp'), may hold values from -0.125 to 0.125
- a_in: bfloat16 [64, 2048, 48], P('grp', 'tp'), may hold values from -0.125 to 0.125
- b_in: bfloat16 [64, 3, 16, 2048], P('grp', None, None, 'tp'), may hold values from -1.5 to 1.5
- a_out: bfloat16 [64, 2048, 16], P('grp', 'tp'), may hold values from -0.125 to 0.125
- b_out: bfloat16 [64, 16, 2048], P('grp', None, 'tp'), may hold values from -1.5 to 1.5
- req_len: int32 [32, 4], replicated, may hold values from 1 to 512, 1024 in all within a row
- req_adapter: int32 [32, 4], replicated, may hold values from 0 to 63, as said below
- holder: int32 [64], replicated, may hold values from 0 to 63, each once
- page_table: int32 [32, 8], P('grp'), may hold values from 0 to 7, each once within a row
Outputs:
- layer_out: bfloat16 [32768, 2048], P('grp', 'tp')
- kv_pages: bfloat16 [256, 2, 128, 2048], P('grp', None, None, 'tp')
Inputs may be any that keep to these rules, and one draw needn't show every extreme that they name: `req_adapter`: exactly 16 different adapters appear among all requests.
All inputs are finite; a program needn't handle non-finite values.
Results may differ from a plain program's by a relative error of at most 0.017.
The roundings to bfloat16 on the way count: a program that leaves them out, or rounds other values in their place, can miss the bound.
Values may be sent and summed in bfloat16 or wider, within the bound.
No kernel may reach another device: no remote copies, remote signals or barrier semaphores. Data moves between devices by JAX's collectives and lax.ppermute only.
A program may use at most 128 MiB of HBM per device.

v0:
```python
import math
import jax
import jax.numpy as jnp
from jax import lax
from jax.sharding import PartitionSpec as P

HD = 128
PAGE = 128
EPSILON = 1e-05
THETA = 10000.0


def shifted(block, axis, distance):
    devices = range(lax.axis_size(axis))
    route = [(i - distance, i) for i in devices if i - distance in devices]
    return lax.ppermute(block, axis, route)


USED = 16


def xor_allreduce(value, axis):
    count = lax.axis_size(axis)
    step = 1
    while step < count:
        route = [(i, i ^ step) for i in range(count)]
        value = value + lax.ppermute(value, axis, route)
        step *= 2
    return value


def fetch_adapters(stores, req_adapter, holder, wanted, group_id):
    held = stores[0].shape[0]
    total = holder.shape[0]
    names = jnp.arange(total, dtype=jnp.int32)
    used = jnp.any(req_adapter.reshape(-1)[:, None] == names[None, :], axis=0)
    rank = jnp.cumsum(used.astype(jnp.int32)) - 1
    picks = jnp.arange(USED, dtype=jnp.int32)
    hit = used[None, :] & (rank[None, :] == picks[:, None])
    chosen = jnp.sum(jnp.where(hit, names[None, :], 0), axis=1)
    slots = holder[chosen]
    mine = slots // held == group_id
    local_idx = slots % held
    flat = jnp.concatenate([s.reshape(held, -1) for s in stores], axis=1)
    compact = jnp.where(mine[:, None], jnp.take(flat, local_idx, axis=0), jnp.zeros((), flat.dtype))
    compact = lax.psum(compact, "grp")
    mine_rows = jnp.take(compact, rank[wanted], axis=0)
    out = []
    at = 0
    for s in stores:
        size = math.prod(s.shape[1:])
        out.append(mine_rows[:, at : at + size].reshape((wanted.shape[0],) + s.shape[1:]))
        at += size
    return tuple(out)


def rms_norm(token_rows, norm_gain):
    values = token_rows.astype(jnp.float32)
    norm_scale = lax.rsqrt(jnp.mean(values * values, axis=-1, keepdims=True) + EPSILON)
    return (values * norm_scale * norm_gain).astype(jnp.bfloat16)


def request_layout(lengths, offset, tok_count):
    end_at = jnp.cumsum(lengths)
    starts = end_at - lengths
    row_ids = jnp.arange(tok_count, dtype=jnp.int32)
    segment = jnp.sum((row_ids[:, None] >= end_at[None, :]).astype(jnp.int32), axis=1)
    member = segment[:, None] == jnp.arange(lengths.shape[0], dtype=jnp.int32)[None, :]
    begin_at = jnp.sum(jnp.where(member, starts[None, :], 0), axis=1)
    position = row_ids - begin_at + jnp.where(segment == 0, offset, 0)
    return (segment, member, position)


def rotate(head_rows, position, head_dim):
    half_dim = head_dim // 2
    frequency = THETA ** (-(jnp.arange(half_dim, dtype=jnp.float32) * (2.0 / head_dim)))
    angles = position.astype(jnp.float32)[:, None] * frequency[None, :]
    cosine = jnp.cos(angles)[:, None, :]
    sine_part = jnp.sin(angles)[:, None, :]
    lower_half = head_rows[..., :half_dim]
    upper_half = head_rows[..., half_dim:]
    return jnp.concatenate(
        [
            lower_half * cosine - upper_half * sine_part,
            upper_half * cosine + lower_half * sine_part,
        ],
        axis=-1,
    )


def local(
    tokens,
    norm_gain,
    w_qkv,
    w_out,
    a_in,
    b_in,
    a_out,
    b_out,
    req_len,
    req_adapter,
    holder,
    page_table,
):
    tok_count = tokens.shape[0]
    local_width = w_out.shape[0]
    local_heads = local_width // HD
    req_count = req_len.shape[1]
    rank_dim = a_out.shape[2]
    group_id = lax.axis_index("grp")
    tp_id = lax.axis_index("tp")
    lengths = lax.dynamic_index_in_dim(req_len, group_id, 0, keepdims=False)
    earlier = lax.dynamic_index_in_dim(req_len, jnp.maximum(group_id - 1, 0), 0, keepdims=False)
    continued = group_id > 0
    prev_len = earlier[req_count - 1]
    offset = jnp.where(continued, prev_len, 0)
    segment, member, position = request_layout(lengths, offset, tok_count)
    wanted = lax.dynamic_index_in_dim(req_adapter, group_id, 0, keepdims=False)
    sel_in, sel_up, sel_odown, sel_oup = fetch_adapters(
        (a_in, b_in, a_out, b_out), req_adapter, holder, wanted, group_id
    )
    member_f = member.astype(jnp.float32)
    pick_bf = member.astype(jnp.bfloat16)
    normed = rms_norm(tokens, norm_gain)
    own_cols = lax.dynamic_slice_in_dim(normed, tp_id * local_width, local_width, 1)
    down_f = jnp.einsum("td,rdk->trk", own_cols, sel_in, preferred_element_type=jnp.float32)
    lowrank_f = xor_allreduce(jnp.sum(down_f * member_f[:, :, None], axis=1), "tp")
    lowrank = lowrank_f.astype(jnp.bfloat16)
    spread = (pick_bf[:, :, None] * lowrank[:, None, :]).reshape(tok_count, req_count, 3, rank_dim)
    delta_qkv = jnp.einsum("trck,rckd->tcd", spread, sel_up, preferred_element_type=jnp.float32)
    base_qkv = jnp.dot(
        normed, w_qkv.reshape(w_qkv.shape[0], 3 * local_width), preferred_element_type=jnp.float32
    )
    qkv = (base_qkv.reshape(tok_count, 3, local_width) + delta_qkv).reshape(
        tok_count, 3, local_heads, HD
    )
    query_rows = rotate(qkv[:, 0], position, HD).astype(jnp.bfloat16)
    key_rows = rotate(qkv[:, 1], position, HD).astype(jnp.bfloat16).reshape(tok_count, local_width)
    value_rows = qkv[:, 2].astype(jnp.bfloat16).reshape(tok_count, local_width)
    row_ids = jnp.arange(tok_count, dtype=jnp.int32)
    far_key, far_value = shifted((key_rows, value_rows), "grp", 1)
    far_ok = continued & (segment[:, None] == 0) & (row_ids[None, :] >= tok_count - prev_len)
    far_count = far_key.shape[0]
    near_ok = (segment[:, None] == segment[None, :]) & (row_ids[None, :] <= row_ids[:, None])
    allowed = jnp.concatenate([far_ok, near_ok], axis=1)
    key_all = jnp.concatenate([far_key, key_rows], axis=0).reshape(
        far_count + tok_count, local_heads, HD
    )
    value_all = jnp.concatenate([far_value, value_rows], axis=0).reshape(
        far_count + tok_count, local_heads, HD
    )
    score_scale = 1.0 / math.sqrt(HD)
    scores = (
        jnp.einsum("thd,shd->hts", query_rows, key_all, preferred_element_type=jnp.float32)
        * score_scale
    )
    scores = jnp.where(allowed[None], scores, -jnp.inf)
    row_top = jnp.max(scores, axis=-1, keepdims=True)
    weights = jnp.exp(scores - row_top)
    weights_bf = (weights / jnp.sum(weights, axis=-1, keepdims=True)).astype(jnp.bfloat16)
    mixed_heads = jnp.einsum(
        "hts,shd->thd", weights_bf, value_all, preferred_element_type=jnp.float32
    )
    attended = mixed_heads.astype(jnp.bfloat16).reshape(tok_count, local_width)
    partial_value = jnp.dot(attended, w_out, preferred_element_type=jnp.float32)
    down_o = jnp.einsum("td,rdk->trk", attended, sel_odown, preferred_element_type=jnp.float32)
    low_part = jnp.sum(down_o * member_f[:, :, None], axis=1).astype(jnp.bfloat16)
    n_tp = lax.axis_size("tp")
    packed = jnp.concatenate(
        [
            partial_value.astype(jnp.bfloat16).reshape(tok_count, n_tp, local_width),
            jnp.broadcast_to(low_part[:, None, :], (tok_count, n_tp, rank_dim)),
        ],
        axis=2,
    ).reshape(tok_count, n_tp * (local_width + rank_dim))
    summed = lax.psum_scatter(packed, "tp", scatter_dimension=1, tiled=True)
    base_out = summed[:, :local_width].astype(jnp.float32)
    low_o = summed[:, local_width:]
    spread_o = (pick_bf[:, :, None] * low_o[:, None, :]).reshape(tok_count, req_count * rank_dim)
    delta_o = jnp.dot(
        spread_o,
        sel_oup.reshape(req_count * rank_dim, local_width),
        preferred_element_type=jnp.float32,
    )
    own_rows = lax.dynamic_slice_in_dim(tokens, tp_id * local_width, local_width, 1).astype(
        jnp.float32
    )
    layer_out = (own_rows + base_out + delta_o).astype(jnp.bfloat16)
    page_row = page_table[0]
    page_count = page_row.shape[0]
    numbers = jnp.arange(page_count, dtype=jnp.int32)
    inverse = jnp.sum(jnp.where(page_row[:, None] == numbers[None, :], numbers[:, None], 0), axis=0)
    both_blocks = jnp.stack(
        [
            key_rows.reshape(page_count, PAGE, local_width),
            value_rows.reshape(page_count, PAGE, local_width),
        ],
        axis=1,
    )
    kv_pages = jnp.take(both_blocks, inverse, axis=0)
    return (layer_out, kv_pages)


def solution(mesh):
    return jax.shard_map(
        local,
        mesh=mesh,
        in_specs=(
            P("grp", None),
            P(),
            P(None, None, "tp"),
            P("tp", None),
            P("grp", "tp", None),
            P("grp", None, None, "tp"),
            P("grp", "tp", None),
            P("grp", None, "tp"),
            P(),
            P(),
            P(),
            P("grp", None),
        ),
        out_specs=(P("grp", "tp"), P("grp", None, None, "tp")),
        check_vma=False,
    )
```

profile of v0, /device:TPU:4, one launch (start us, length us, event | category | flops | bytes accessed | tf_op | source)
XLA Modules:
  0.0 312.4 jit_solution(5977130857267515130)
XLA Ops:
  7.2 0.8 copy.93
  8.0 0.8 copy.63
  9.5 1.3 gather_fusion.1
  10.9 0.8 copy.92
  11.7 0.9 copy.65
  12.8 0.8 copy.66
  14.0 1.2 gather_fusion.2
  15.3 1.2 select_select_fusion
  17.1 0.6 fusion.11
  17.7 0.5 slice.46
  19.6 3.1 fusion.2
  22.7 0.6 gather_fusion
  23.4 4.7 %copy.62 = bf16[2048,3,256]{0,2,1:T(8,128)(2,1)} copy(bf16[2048,3,256]{2,0,1:T(8,128)(2,1)} %param.14) | data formatting | bytes 6291456 | tf_op args[2]
  28.1 0.5 broadcast_and_fusion
  28.6 3.5 %fusion.4 = bf16[1024,2048]{1,0:T(8,128)(2,1)S(1)} fusion(bf16[1024,2048]{1,0:T(8,128)(2,1)} %param.12, f32[2048]{0:T(1024)S(1)} %copy-done.7, f32[1024]{0:T(1024)S(1)} %add_rsqrt_fusion), kind=kLoop, calls=%fused_computation.14 | loop fusion | flops 8388608 | bytes 8400896 | tf_op jit(solution)/shard_map/convert_element_type | solution.py:60
  32.2 1.9 copy-done.2
  34.1 5.1 %fusion.9 = f32[1024,3,256]{0,2,1:T(8,128)} fusion(bf16[1024,2048]{1,0:T(8,128)(2,1)S(1)} %fusion.4, bf16[2048,3,256]{0,2,1:T(8,128)(2,1)S(1)} %copy-done.3), kind=kOutput, calls=%fused_computation.21 | convolution fusion | flops 3221225472 | bytes 10485760 | tf_op jit(solution)/shard_map/dot_general | solution.py:131
  39.2 129.0 %all-reduce.2.cloned.1.call-done = bf16[16,32768]{1,0:T(8,128)(2,1)} async-done(((bf16[16,32768]{1,0:T(8,128)(2,1)}), bf16[16,32768]{1,0:T(8,128)(2,1)}) %all-reduce.2.cloned.1.call-update) | async-done | bytes 1048592 | tf_op jit(solution)/shard_map/psum | solution.py:46
  168.2 2.4 gather_fusion.3
  170.8 0.7 copy-done.5
  171.5 0.7 fusion.48
  172.2 0.2 reshape.421
  172.6 1.4 fusion.21
  174.2 1.5 pad_add_fusion
  175.7 1.6 collective-permute-start.1
  177.3 3.0 multiply_cosine_fusion
  180.3 2.8 collective-permute-done.1
  183.1 3.3 %collective-permute-start.2 = (f32[1024,48]{0,1:T(8,128)S(1)}, f32[1024,48]{0,1:T(8,128)S(1)}, u32[]{:S(2)}, u32[]{:S(2)}) collective-permute-start(f32[1024,48]{0,1:T(8,128)S(1)} %add.163), channel_id=1, source_target_pairs={{0,4},{1,5},{2,6},{3,7},{4,0},{5,1},{6,2},{7,3},{8,12},{9,13},{10,... | collective-permute-start | bytes 589832 | tf_op jit(solution)/shard_map/ppermute | solution.py:27
  186.4 0.8 fusion.47
  187.2 0.2 reshape.426
  187.6 3.7 %collective-permute-done.2 = f32[1024,48]{0,1:T(8,128)S(1)} collective-permute-done((f32[1024,48]{0,1:T(8,128)S(1)}, f32[1024,48]{0,1:T(8,128)S(1)}, u32[]{:S(2)}, u32[]{:S(2)}) %collective-permute-start.2) | collective-permute-done | bytes 196640 | tf_op jit(solution)/shard_map/ppermute | solution.py:27
  191.3 2.5 bitcast_add_fusion
  193.8 0.9 slice.89
  194.8 0.9 copy-done.1
  195.6 1.2 fusion.46
  196.8 0.3 copy.88
  197.1 3.2 %collective-permute-start.3 = (bf16[1024,256]{0,1:T(8,128)(2,1)}, bf16[1024,256]{0,1:T(8,128)(2,1)}, u32[]{:S(2)}, u32[]{:S(2)}) collective-permute-start(bf16[1024,256]{0,1:T(8,128)(2,1)} %bitcast.106), channel_id=1, source_target_pairs={{0,8},{8,16},{16,24},{24,32},{32,40},{40,48},{48,56},{56,64},{64,7... | collective-permute-start | bytes 1572872 | tf_op jit(solution)/shard_map/ppermute | solution.py:16
  200.3 1.6 copy.89
  201.9 1.6 multiply_subtract_fusion
  203.5 0.3 maximum_convert_fusion
  203.8 1.0 copy.71
  204.8 4.1 %collective-permute-start.4 = (bf16[1024,256]{0,1:T(8,128)(2,1)}, bf16[1024,256]{0,1:T(8,128)(2,1)}, u32[]{:S(2)}, u32[]{:S(2)}) collective-permute-start(bf16[1024,256]{0,1:T(8,128)(2,1)} %bitcast.29), channel_id=1, source_target_pairs={{0,8},{8,16},{16,24},{24,32},{32,40},{40,48},{48,56},{56,64},{64,7... | collective-permute-start | bytes 1572872 | tf_op jit(solution)/shard_map/ppermute | solution.py:16
  209.0 1.3 slice_bitcast_fusion
  210.3 2.6 subtract_convert_fusion
  212.9 10.3 %collective-permute-done.4 = bf16[1024,256]{0,1:T(8,128)(2,1)} collective-permute-done((bf16[1024,256]{0,1:T(8,128)(2,1)}, bf16[1024,256]{0,1:T(8,128)(2,1)}, u32[]{:S(2)}, u32[]{:S(2)}) %collective-permute-start.4) | collective-permute-done | bytes 524320 | tf_op jit(solution)/shard_map/ppermute | solution.py:16
  223.2 1.3 copy.72
  224.5 10.8 %fusion.49 = (f32[2,1024]{1,0:T(2,128)S(1)}, f32[2,1024,2048]{2,1,0:T(8,128)}) fusion(pred[1024,2048]{1,0:T(8,128)(4,1)} %pad_add_fusion, bf16[1024,2,128]{2,0,1:T(8,128)(2,1)S(1)} %maximum_convert_fusion, bf16[1024,2,128]{2,0,1:T(8,128)(2,1)S(1)} %copy.72, bf16[1024,2,64]{2,0,1:T(8,128)(2,1)} %get-tuple-element.7, bf16[1024,2,64]{2,0,1:T(8,128)(2,1)} %get-tuple-element.6), kind=kOutput, calls=%fused_computation.127 | convolution fusion | flops 1093666816 | bytes 20455424 | tf_op jit(solution)/shard_map/sub | solution.py:159
  235.3 8.9 %fusion.16 = bf16[2,128,1024]{2,1,0:T(8,128)(2,1)S(1)} fusion(f32[2,1024,2048]{2,1,0:T(8,128)} %get-tuple-element.23, f32[2,1024]{1,0:T(2,128)S(1)} %get-tuple-element.22, bf16[1024,2,128]{0,2,1:T(8,128)(2,1)S(1)} %slice_bitcast_fusion, bf16[1024,2,128]{0,2,1:T(8,128)(2,1)} %bitcast.22), kind=kOutput, calls=%fused_computation.32 | convolution fusion | flops 1084489728 | bytes 18358272 | tf_op jit(solution)/shard_map/hts,shd->thd/dot_general | solution.py:161
  244.2 0.2 fusion.50
  244.5 3.2 %convolution_convert_fusion = bf16[1024,2048]{1,0:T(8,128)(2,1)} fusion(bf16[1024,256]{0,1:T(8,128)(2,1)S(1)} %bitcast.104, bf16[256,2048]{1,0:T(8,128)(2,1)S(1)} %copy-done), kind=kOutput, calls=%fused_computation.25 | convolution fusion | flops 1075838976 | bytes 5767168 | tf_op jit(solution)/shard_map/dot_general | solution.py:165
  247.7 6.4 %copy.82 = bf16[1024,2048]{0,1:T(8,128)(2,1)} copy(bf16[1024,2048]{1,0:T(8,128)(2,1)} %convolution_convert_fusion) | data formatting | bytes 8388608 | tf_op jit(solution)/shard_map/reshape | solution.py:171
  254.1 4.7 %pad_maximum_fusion = bf16[1024,8,272]{0,2,1:T(8,128)(2,1)} fusion(bf16[1024,8,16]{0,2,1:T(8,128)(2,1)S(1)} %broadcast_in_dim.158, bf16[1024,8,256]{0,2,1:T(8,128)(2,1)} %bitcast.97), kind=kLoop, calls=%fused_computation.20 | loop fusion | flops 8912896 | bytes 8912896 | tf_op jit(solution)/shard_map/concatenate | solution.py:169
  258.9 0.6 copy-done.10
  259.6 0.5 copy.83
  260.3 0.3 copy.80
  260.6 1.1 reshape.475
  261.8 1.1 pad_maximum_fusion.2
  262.9 0.6 gather_fusion.4
  263.5 1.1 broadcast_select_fusion
  264.7 36.7 %reduce-scatter.4.cloned.1.call-done = bf16[272,1024]{1,0:T(8,128)(2,1)} async-done(((bf16[2176,1024]{1,0:T(8,128)(2,1)}), bf16[272,1024]{1,0:T(8,128)(2,1)}) %reduce-scatter.4.cloned.1.call-update) | async-done | bytes 557072
  301.3 0.8 slice.78
  302.1 1.1 slice.77
  303.2 0.2 copy.90
  303.4 2.2 fusion.15
  (74 shorter events, 3.0 us)
Async XLA Ops:
  7.2 237.3 %copy-start = (bf16[256,2048]{1,0:T(8,128)(2,1)S(1)}, bf16[256,2048]{1,0:T(8,128)(2,1)}, u32[]{:S(2)}) copy-start(bf16[256,2048]{1,0:T(8,128)(2,1)} %param.15) | copy-start | bytes 3145732
  7.2 161.0 %all-reduce.2.cloned.1.call-start = ((), (), s32[]{:S(2)}) async-start(), calls=%async_computation.1 | async-start | bytes 2097152 | tf_op jit(solution)/shard_map/psum | solution.py:46
  14.0 2.5 copy-start.8
  14.0 2.5 copy-start.9
  16.4 284.9 %reduce-scatter.4.cloned.1.call-start = ((), (), s32[]{:S(2)}) async-start(), calls=%async_computation.2 | async-start | bytes 5013504
  22.7 5.9 %copy-start.7 = (f32[2048]{0:T(1024)S(1)}, f32[2048]{0:T(1024)}, u32[]{:S(2)}) copy-start(f32[2048]{0:T(1024)} %param.13) | copy-start | bytes 24580
  28.6 5.4 %copy-start.3 = (bf16[2048,3,256]{0,2,1:T(8,128)(2,1)S(1)}, bf16[2048,3,256]{0,2,1:T(8,128)(2,1)}, u32[]{:S(2)}) copy-start(bf16[2048,3,256]{0,2,1:T(8,128)(2,1)} %copy.62) | copy-start | bytes 9437188
  32.1 1.9 copy-start.2
  170.8 0.7 copy-start.5
  172.6 14.6 %copy-start.6 = (bf16[4,12288]{1,0:T(4,128)(2,1)S(1)}, bf16[4,12288]{1,0:T(4,128)(2,1)}, u32[]{:S(2)}) copy-start(bf16[4,12288]{1,0:T(4,128)(2,1)} %get-tuple-element.13) | copy-start | bytes 294916
  174.1 1.6 collective-permute-start
  175.7 7.4 %collective-permute-start.1 = (f32[1024,48]{0,1:T(8,128)S(1)}, f32[1024,48]{0,1:T(8,128)S(1)}, u32[]{:S(2)}, u32[]{:S(2)}) collective-permute-start(f32[1024,48]{0,1:T(8,128)S(1)} %add.162), channel_id=1, source_target_pairs={{0,2},{1,3},{2,0},{3,1},{4,6},{5,7},{6,4},{7,5},{8,10},{9,11},{10,... | collective-permute-start | bytes 589832 | tf_op jit(solution)/shard_map/ppermute | solution.py:27
  183.1 8.2 %collective-permute-start.2 = (f32[1024,48]{0,1:T(8,128)S(1)}, f32[1024,48]{0,1:T(8,128)S(1)}, u32[]{:S(2)}, u32[]{:S(2)}) collective-permute-start(f32[1024,48]{0,1:T(8,128)S(1)} %add.163), channel_id=1, source_target_pairs={{0,4},{1,5},{2,6},{3,7},{4,0},{5,1},{6,2},{7,3},{8,12},{9,13},{10,... | collective-permute-start | bytes 589832 | tf_op jit(solution)/shard_map/ppermute | solution.py:27
  193.8 1.8 copy-start.1
  197.1 38.1 %collective-permute-start.3 = (bf16[1024,256]{0,1:T(8,128)(2,1)}, bf16[1024,256]{0,1:T(8,128)(2,1)}, u32[]{:S(2)}, u32[]{:S(2)}) collective-permute-start(bf16[1024,256]{0,1:T(8,128)(2,1)} %bitcast.106), channel_id=1, source_target_pairs={{0,8},{8,16},{16,24},{24,32},{32,40},{40,48},{48,56},{56,64},{64,7... | collective-permute-start | bytes 1572872 | tf_op jit(solution)/shard_map/ppermute | solution.py:16
  204.8 18.3 %collective-permute-start.4 = (bf16[1024,256]{0,1:T(8,128)(2,1)}, bf16[1024,256]{0,1:T(8,128)(2,1)}, u32[]{:S(2)}, u32[]{:S(2)}) collective-permute-start(bf16[1024,256]{0,1:T(8,128)(2,1)} %bitcast.29), channel_id=1, source_target_pairs={{0,8},{8,16},{16,24},{24,32},{32,40},{40,48},{48,56},{56,64},{64,7... | collective-permute-start | bytes 1572872 | tf_op jit(solution)/shard_map/ppermute | solution.py:16
  258.8 0.7 copy-start.10
  258.8 1.3 copy-start.4
Sparse Core Ops, SparseCore 0:
  16.6 151.6 all-reduce.1
  259.0 42.3 reduce-scatter.3
where the time goes:
time: 314 us; the launch traced here: 312 us
  waiting for transfers between devices  183 us (58%)
  local copies, waits for them, and re-layouts  40.9 us (13%)
  matrix products  34.3 us (11%)
  other arithmetic  26.4 us (8%)
  between operations  15.9 us (5%)
  starting transfers between devices  12.3 us (4%)
    psum x1, waiting for transfers between devices, fetch_adapters(): compact = lax.psum(compact, 'grp')  129 us
    unnamed x3, waiting for transfers between devices  36.7 us
    unnamed x34, local copies, waits for them, and re-layouts  15.3 us
    sub x1, matrix products, local(): weights = jnp.exp(scores - row_top)  10.8 us
    ppermute x2, waiting for transfers between devices, shifted(): return lax.ppermute(block, axis, route)  10.3 us
    dot_general x1, matrix products, local(): jnp.einsum('hts,shd->thd', weights_bf, value_all, preferred_element_type=...  8.93 us
    ppermute x2, starting transfers between devices, shifted(): return lax.ppermute(block, axis, route)  7.3 us
    ppermute x3, waiting for transfers between devices, xor_allreduce(): value = value + lax.ppermute(value, axis, route)  6.53 us
  transfers between devices with their start and end apart: 7, of which 5 were waited for; matrix products, arithmetic and copies ran while one was open for 16% of the time, Pallas kernels for 0%

commit v1 on v0

--- a/solution.py
+++ b/solution.py
@@ -1,3 +1,4 @@
+import functools
 import math
 import jax
 import jax.numpy as jnp
@@ -8,6 +9,14 @@
 PAGE = 128
 EPSILON = 1e-05
 THETA = 10000.0
+
+
+def hold_groups_now(inputs, mesh_ax):
+    r2 = jnp.sum(jax.lax.all_gather(inputs, mesh_ax), 0)
+    return r2
+
+
+_switch_rates = functools.partial(hold_groups_now, mesh_ax="grp")
 
 
 def shifted(block, axis, distance):
@@ -43,7 +52,7 @@
     local_idx = slots % held
     flat = jnp.concatenate([s.reshape(held, -1) for s in stores], axis=1)
     compact = jnp.where(mine[:, None], jnp.take(flat, local_idx, axis=0), jnp.zeros((), flat.dtype))
-    compact = lax.psum(compact, "grp")
+    compact = _switch_rates(compact)
     mine_rows = jnp.take(compact, rank[wanted], axis=0)
     out = []
     at = 0

time: 314 us -> 400 us (1.27)
  waiting for transfers between devices: 183 us -> 262 us
  other arithmetic: 26.4 us -> 34 us
    all_gather x0 -> x1, waiting for transfers between devices: none -> 213 us  [hold_groups_now(): r2 = jnp.sum(jax.lax.all_gather(inputs, mesh_ax), 0)]
    psum x1 -> x0, waiting for transfers between devices: 129 us -> none  [fetch_adapters(): compact = lax.psum(compact, 'grp')]
    reduce_sum x0 -> x1, other arithmetic: none -> 11.4 us  [hold_groups_now(): r2 = jnp.sum(jax.lax.all_gather(inputs, mesh_ax), 0)]
    ppermute x2, waiting for transfers between devices: 10.3 us -> 4.58 us  [shifted(): return lax.ppermute(block, axis, route)]
    unnamed x34 -> x42, local copies, waits for them, and re-layouts: 15.3 us -> 16.6 us
  transfers between devices with their start and end apart: 7 -> 7, of which waited for: 5 -> 5; matrix products, arithmetic and copies ran while one was open for 16% -> 12% of each run, Pallas kernels for 0% -> 0%
where the time goes in v1:
time: 400 us; the launch traced here: 399 us
  waiting for transfers between devices  262 us (66%)
  local copies, waits for them, and re-layouts  41.7 us (10%)
  matrix products  34.3 us (9%)
  other arithmetic  34 us (8%)
  between operations  15.9 us (4%)
  starting transfers between devices  11.3 us (3%)
    all_gather x1, waiting for transfers between devices, hold_groups_now(): r2 = jnp.sum(jax.lax.all_gather(inputs, mesh_ax), 0)  213 us
    unnamed x3, waiting for transfers between devices  36.5 us
    unnamed x42, local copies, waits for them, and re-layouts  16.6 us
    reduce_sum x1, other arithmetic, hold_groups_now(): r2 = jnp.sum(jax.lax.all_gather(inputs, mesh_ax), 0)  11.4 us
    sub x1, matrix products, local(): weights = jnp.exp(scores - row_top)  10.8 us
    dot_general x1, matrix products, local(): jnp.einsum('hts,shd->thd', weights_bf, value_all, preferred_element_type=...  8.93 us
  transfers between devices with their start and end apart: 7, of which 5 were waited for; matrix products, arithmetic and copies ran while one was open for 12% of the time, Pallas kernels for 0%

profile of v1, /device:TPU:4, one launch (start us, length us, event | category | flops | bytes accessed | tf_op | source)
XLA Modules:
  0.0 398.9 jit_solution(16586959923026743653)
XLA Ops:
  7.2 0.8 copy.93
  8.0 0.8 copy.66
  9.0 0.8 copy.92
  9.9 0.9 copy.65
  11.0 0.8 copy.63
  12.5 1.3 gather_fusion.1
  14.0 1.2 gather_fusion.2
  15.2 1.2 fusion.20
  16.7 0.6 gather_fusion
  17.6 0.5 slice.46
  19.4 4.7 %copy.62 = bf16[2048,3,256]{0,2,1:T(8,128)(2,1)} copy(bf16[2048,3,256]{2,0,1:T(8,128)(2,1)} %param.14) | data formatting | bytes 6291456 | tf_op args[2]
  24.4 3.2 fusion.2
  27.7 0.5 broadcast_and_fusion
  28.2 1.6 fusion.11
  29.8 1.0 fusion.4
  30.8 2.0 copy-done.3
  32.9 5.1 %fusion.9 = f32[1024,3,256]{0,2,1:T(8,128)} fusion(bf16[1024,2048]{1,0:T(8,128)(2,1)S(1)} %fusion.4, bf16[2048,3,256]{0,2,1:T(8,128)(2,1)S(1)} %copy-done.6), kind=kOutput, calls=%fused_computation.21 | convolution fusion | flops 3221225472 | bytes 10485760 | tf_op jit(solution)/shard_map/dot_general | solution.py:140
  38.0 212.9 %all-gather.2.cloned.1.call-done = bf16[32,16,32768]{2,1,0:T(8,128)(2,1)} async-done(((bf16[1,16,32768]{2,1,0:T(8,128)(2,1)}), bf16[32,16,32768]{2,1,0:T(8,128)(2,1)}) %all-gather.2.cloned.1.call-update) | async-done | bytes 33554448 | tf_op jit(solution)/shard_map/all_gather | solution.py:15
  250.9 11.4 %reduce_sum.91 = bf16[16,32768]{1,0:T(8,128)(2,1)S(1)} reduce(bf16[32,16,32768]{2,1,0:T(8,128)(2,1)} %all-gather.2.cloned.1.call-done, bf16[]{:T(256)} %constant.124.clone.1), dimensions={0}, to_apply=%region_4.5 | reduce | flops 16252928 | bytes 34603008 | tf_op jit(solution)/shard_map/reduce_sum | solution.py:15
  262.2 0.8 gather_fusion.3
  263.3 0.7 copy-done.8
  264.0 0.7 fusion.49
  264.7 0.2 reshape.466
  265.0 1.4 fusion.22
  266.6 1.5 pad_add_fusion
  268.2 1.8 collective-permute-start.1
  269.9 1.9 multiply_cosine_fusion
  271.8 3.9 collective-permute-done.1
  275.8 3.1 collective-permute-start.2
  278.9 0.8 fusion.48
  279.7 0.2 reshape.471
  280.0 3.7 collective-permute-done.2
  283.8 2.5 bitcast_add_fusion
  286.3 1.5 fusion.47
  287.8 0.8 copy-done.2
  288.6 0.9 slice.89
  289.4 1.5 copy.89
  291.0 0.4 multiply_subtract_fusion
  291.4 0.3 maximum_convert_fusion
  291.7 1.0 copy.71
  292.7 2.8 collective-permute-start.4
  295.5 1.6 copy.88
  297.1 3.5 collective-permute-start.3
  300.6 2.1 slice_bitcast_fusion
  302.7 2.5 subtract_convert_fusion
  305.2 4.6 %collective-permute-done.4 = bf16[1024,256]{0,1:T(8,128)(2,1)} collective-permute-done((bf16[1024,256]{0,1:T(8,128)(2,1)}, bf16[1024,256]{0,1:T(8,128)(2,1)}, u32[]{:S(2)}, u32[]{:S(2)}) %collective-permute-start.4) | collective-permute-done | bytes 524320 | tf_op jit(solution)/shard_map/ppermute | solution.py:25
  309.7 1.3 copy.72
  311.1 10.8 %fusion.50 = (f32[2,1024]{1,0:T(2,128)S(1)}, f32[2,1024,2048]{2,1,0:T(8,128)}) fusion(pred[1024,2048]{1,0:T(8,128)(4,1)} %pad_add_fusion, bf16[1024,2,128]{2,0,1:T(8,128)(2,1)S(1)} %maximum_convert_fusion, bf16[1024,2,128]{2,0,1:T(8,128)(2,1)S(1)} %copy.72, bf16[1024,2,64]{2,0,1:T(8,128)(2,1)} %get-tuple-element.7, bf16[1024,2,64]{2,0,1:T(8,128)(2,1)} %get-tuple-element.6), kind=kOutput, calls=%fused_computation.128 | convolution fusion | flops 1093666816 | bytes 20455424 | tf_op jit(solution)/shard_map/sub | solution.py:168
  321.9 8.9 %fusion.16 = bf16[2,128,1024]{2,1,0:T(8,128)(2,1)S(1)} fusion(f32[2,1024,2048]{2,1,0:T(8,128)} %get-tuple-element.23, f32[2,1024]{1,0:T(2,128)S(1)} %get-tuple-element.22, bf16[1024,2,128]{0,2,1:T(8,128)(2,1)S(1)} %copy-done.9, bf16[1024,2,128]{0,2,1:T(8,128)(2,1)} %bitcast.23), kind=kOutput, calls=%fused_computation.32 | convolution fusion | flops 1084489728 | bytes 18358272 | tf_op jit(solution)/shard_map/hts,shd->thd/dot_general | solution.py:170
  330.8 0.2 fusion.51
  331.1 3.2 convolution_convert_fusion
  334.3 6.4 %copy.82 = bf16[1024,2048]{0,1:T(8,128)(2,1)} copy(bf16[1024,2048]{1,0:T(8,128)(2,1)} %convolution_convert_fusion) | data formatting | bytes 8388608 | tf_op jit(solution)/shard_map/reshape | solution.py:180
  340.8 4.7 %pad_maximum_fusion = bf16[1024,8,272]{0,2,1:T(8,128)(2,1)} fusion(bf16[1024,8,16]{0,2,1:T(8,128)(2,1)S(1)} %broadcast_in_dim.158, bf16[1024,8,256]{0,2,1:T(8,128)(2,1)} %bitcast.101), kind=kLoop, calls=%fused_computation.20 | loop fusion | flops 8912896 | bytes 8912896 | tf_op jit(solution)/shard_map/concatenate | solution.py:178
  345.5 0.6 copy-done.14
  346.3 0.5 copy.83
  346.9 0.3 copy.80
  347.3 1.1 reshape.520
  348.4 1.1 pad_maximum_fusion.2
  349.5 0.6 gather_fusion.4
  350.2 1.1 broadcast_select_fusion
  351.3 36.5 %reduce-scatter.4.cloned.1.call-done = bf16[272,1024]{1,0:T(8,128)(2,1)} async-done(((bf16[2176,1024]{1,0:T(8,128)(2,1)}), bf16[272,1024]{1,0:T(8,128)(2,1)}) %reduce-scatter.4.cloned.1.call-update) | async-done | bytes 557072
  387.8 0.8 slice.78
  388.6 1.1 slice.77
  389.9 2.2 fusion.15
  (83 shorter events, 3.2 us)
Async XLA Ops:
  7.2 323.9 %copy-start = (bf16[256,2048]{1,0:T(8,128)(2,1)S(1)}, bf16[256,2048]{1,0:T(8,128)(2,1)}, u32[]{:S(2)}) copy-start(bf16[256,2048]{1,0:T(8,128)(2,1)} %param.15) | copy-start | bytes 3145732
  7.2 243.7 %all-gather.2.cloned.1.call-start = ((), (), s32[]{:S(2)}) async-start(), calls=%async_computation.1 | async-start | bytes 34603008 | tf_op jit(solution)/shard_map/all_gather | solution.py:15
  14.0 2.5 copy-start.12
  14.0 2.5 copy-start.13
  16.4 371.4 %reduce-scatter.4.cloned.1.call-start = ((), (), s32[]{:S(2)}) async-start(), calls=%async_computation.2 | async-start | bytes 5013504
  24.2 5.6 %copy-start.11 = (f32[2048]{0:T(1024)S(1)}, f32[2048]{0:T(1024)}, u32[]{:S(2)}) copy-start(f32[2048]{0:T(1024)} %param.13) | copy-start | bytes 24580
  24.2 5.6 %copy-start.1 = (bf16[1024,2048]{1,0:T(8,128)(2,1)S(1)}, bf16[1024,2048]{1,0:T(8,128)(2,1)}, u32[]{:S(2)}) copy-start(bf16[1024,2048]{1,0:T(8,128)(2,1)} %param.12) | copy-start | bytes 12582916
  29.8 3.1 copy-start.6
  30.8 2.0 copy-start.3
  263.1 3.6 copy-start.5
  263.2 0.7 copy-start.8
  266.4 13.6 %copy-start.10 = (bf16[4,12288]{1,0:T(4,128)(2,1)S(1)}, bf16[4,12288]{1,0:T(4,128)(2,1)}, u32[]{:S(2)}) copy-start(bf16[4,12288]{1,0:T(4,128)(2,1)} %get-tuple-element.13) | copy-start | bytes 294916
  266.5 1.7 collective-permute-start
  268.2 7.5 %collective-permute-start.1 = (f32[1024,48]{0,1:T(8,128)S(1)}, f32[1024,48]{0,1:T(8,128)S(1)}, u32[]{:S(2)}, u32[]{:S(2)}) collective-permute-start(f32[1024,48]{0,1:T(8,128)S(1)} %add.160), channel_id=1, source_target_pairs={{0,2},{1,3},{2,0},{3,1},{4,6},{5,7},{6,4},{7,5},{8,10},{9,11},{10,... | collective-permute-start | bytes 589832 | tf_op jit(solution)/shard_map/ppermute | solution.py:36
  271.8 19.2 %copy-start.4 = (f32[1024,64]{1,0:T(8,128)}, f32[1024,64]{1,0:T(8,128)S(1)}, u32[]{:S(2)}) copy-start(f32[1024,64]{1,0:T(8,128)S(1)} %get-tuple-element.15) | copy-start | bytes 786436
  275.8 8.0 %collective-permute-start.2 = (f32[1024,48]{0,1:T(8,128)S(1)}, f32[1024,48]{0,1:T(8,128)S(1)}, u32[]{:S(2)}, u32[]{:S(2)}) collective-permute-start(f32[1024,48]{0,1:T(8,128)S(1)} %add.161), channel_id=1, source_target_pairs={{0,4},{1,5},{2,6},{3,7},{4,0},{5,1},{6,2},{7,3},{8,12},{9,13},{10,... | collective-permute-start | bytes 589832 | tf_op jit(solution)/shard_map/ppermute | solution.py:36
  286.3 2.3 copy-start.2
  292.7 17.0 %collective-permute-start.4 = (bf16[1024,256]{0,1:T(8,128)(2,1)}, bf16[1024,256]{0,1:T(8,128)(2,1)}, u32[]{:S(2)}, u32[]{:S(2)}) collective-permute-start(bf16[1024,256]{0,1:T(8,128)(2,1)} %bitcast.30), channel_id=1, source_target_pairs={{0,8},{8,16},{16,24},{24,32},{32,40},{40,48},{48,56},{56,64},{64,7... | collective-permute-start | bytes 1572872 | tf_op jit(solution)/shard_map/ppermute | solution.py:25
  297.1 24.8 %collective-permute-start.3 = (bf16[1024,256]{0,1:T(8,128)(2,1)}, bf16[1024,256]{0,1:T(8,128)(2,1)}, u32[]{:S(2)}, u32[]{:S(2)}) collective-permute-start(bf16[1024,256]{0,1:T(8,128)(2,1)} %bitcast.110), channel_id=1, source_target_pairs={{0,8},{8,16},{16,24},{24,32},{32,40},{40,48},{48,56},{56,64},{64,7... | collective-permute-start | bytes 1572872 | tf_op jit(solution)/shard_map/ppermute | solution.py:25
  311.1 10.8 %copy-start.9 = (bf16[1024,2,128]{0,2,1:T(8,128)(2,1)S(1)}, bf16[1024,2,128]{0,2,1:T(8,128)(2,1)}, u32[]{:S(2)}) copy-start(bf16[1024,2,128]{0,2,1:T(8,128)(2,1)} %slice_bitcast_fusion) | copy-start | bytes 1572868
  345.5 0.7 copy-start.14
  345.5 1.3 copy-start.7
Sparse Core Ops, SparseCore 0:
  16.5 234.2 all-gather.1
  345.6 42.1 reduce-scatter.3
